TPU v7x, 512 devices: a whole 4x4x16 slice. The times are simulated.
512 devices in a mesh: lon: 32 (over z, x_hi), lat: 16 (over x_lo, y, core).
Axes of the slice: x: 4 (x_hi: 2, x_lo: 2; x = x_hi * 2 + x_lo), y: 4, z: 16, core: 2. Of those that a mesh axis runs over, the one named last changes fastest.
Arguments:
- elevation: float32 [12, 1536, 4096], P(None, 'lat', 'lon'), may hold values from -6 to 6
- equilibrium: float32 [12, 1536, 4096], P(None, 'lat', 'lon'), may hold values from -4 to 4
- transport_u: float32 [12, 1536, 4096], P(None, 'lat', 'lon'), may hold values from -4 to 4
- transport_v: float32 [12, 1536, 4096], P(None, 'lat', 'lon'), may hold values from -4 to 4
- ocean_depth: float32 [1536, 4096], P('lat', 'lon'), may hold values from 0.3 to 3
- bottom_drag: float32 [1536, 4096], P('lat', 'lon'), may hold values from 0.2 to 2
- wet_mask: int32 [1536, 4096], P('lat', 'lon'), may hold values 0 or 1
- lon_green: float32 [4096, 128], P('lon'), may hold values from -0.5 to 0.5
- lat_green: float32 [1536, 49152], P('lat', 'lon'), may hold values from -0.0546875 to 0.0546875
Outputs:
- elevation_next: float32 [12, 1536, 4096], P(None, 'lat', 'lon')
- transport_u_next: float32 [12, 1536, 4096], P(None, 'lat', 'lon')
- transport_v_next: float32 [12, 1536, 4096], P(None, 'lat', 'lon')
All inputs are finite; a program needn't handle non-finite values. No bound on the sum of `wet_mask` on one device may be relied on, other than what follows from the above.
Results may differ from a plain program's by a relative error of at most 0.0001.
Values sent between devices are 32-bit elements; how exact they have to be, the bound alone decides.
No kernel may reach another device: no remote copies, remote signals or barrier semaphores. Data moves between devices by JAX's collectives and lax.ppermute only.
A program may use at most 64 MiB of HBM per device.

v0:
```python
import math
import jax
import jax.numpy as jnp
from jax import lax
from jax.sharding import PartitionSpec as P

FREQS = [1.9323, 2.0, 1.896, 2.0055, 1.0027, 0.9295]
VISCOSITY = 0.5


def extended(array, sides, width, wrap):
    for axis, dim in sides:
        size, length = (lax.axis_size(axis), array.shape[dim])
        up = [(i, (i + 1) % size) for i in range(size if wrap else size - 1)]
        down = [(j, i) for i, j in up]
        last = lax.slice_in_dim(array, length - width, length, axis=dim)
        initial = lax.slice_in_dim(array, 0, width, axis=dim)
        before = lax.ppermute(last, axis, up)
        after = lax.ppermute(initial, axis, down)
        array = jnp.concatenate([before, array, after], axis=dim)
    return array


def row_terms(rows, nlat):
    angle = (-80.0 + 160.0 * (rows.astype(jnp.float32) + 0.5) / nlat) * (math.pi / 180.0)
    return ((1.0 / jnp.cos(angle))[:, None], (2.0 * jnp.sin(angle))[:, None])


def extend(stack, width):
    widened = extended(stack, (("lon", 2),), width, True)
    return extended(widened, (("lat", 1),), width, False)


def slopes(potential_ext, stretch):
    east_slope = (potential_ext[:, 1:-1, 2:] - potential_ext[:, 1:-1, :-2]) * 0.5 * stretch
    north_slope = (potential_ext[:, 2:, 1:-1] - potential_ext[:, :-2, 1:-1]) * 0.5
    return (east_slope, north_slope)


def solve_cells(push_u, push_v, drag_field, wet_frac, coriolis):
    damping = drag_field + 4.0 * VISCOSITY
    frequency = jnp.array(FREQS, jnp.float32)[:, None, None]
    det_real = damping * damping - frequency * frequency + coriolis * coriolis
    det_imag = 2.0 * damping * frequency
    magnitude = det_real * det_real + det_imag * det_imag

    def combine(first, second, factor):
        top_real = damping * first[:6] - frequency * first[6:] + factor * coriolis * second[:6]
        top_imag = damping * first[6:] + frequency * first[:6] + factor * coriolis * second[6:]
        out_real = (top_real * det_real + top_imag * det_imag) / magnitude
        out_imag = (top_imag * det_real - top_real * det_imag) / magnitude
        return wet_frac * jnp.concatenate([out_real, out_imag], axis=0)

    return jnp.concatenate([combine(push_u, push_v, 1.0), combine(push_v, push_u, -1.0)], axis=0)


def relax(flow_ext, east_slope, north_slope, depth_field, drag_field, wet_frac, coriolis):
    beside_all = (
        flow_ext[:, :-2, 1:-1]
        + flow_ext[:, 2:, 1:-1]
        + flow_ext[:, 1:-1, :-2]
        + flow_ext[:, 1:-1, 2:]
    )
    push_u = -depth_field * east_slope + VISCOSITY * beside_all[:12]
    push_v = -depth_field * north_slope + VISCOSITY * beside_all[12:]
    return solve_cells(push_u, push_v, drag_field, wet_frac, coriolis)


def surface(east_ext, north_ext, stretch, wet_frac):
    spread = (east_ext[:, :, 2:] - east_ext[:, :, :-2]) * 0.5 * stretch + (
        north_ext[:, 2:, :] - north_ext[:, :-2, :]
    ) * 0.5
    frequency = jnp.array(FREQS, jnp.float32)[:, None, None]
    return wet_frac * jnp.concatenate([-spread[6:] / frequency, spread[:6] / frequency], axis=0)


def per_device(
    elevation,
    equilibrium,
    transport_u,
    transport_v,
    ocean_depth,
    bottom_drag,
    wet_mask,
    lon_green,
    lat_green,
):
    rows_here = elevation.shape[1]
    total_rows = rows_here * lax.axis_size("lat")
    wet_frac = wet_mask.astype(jnp.float32)
    source = wet_frac * elevation
    mixed = jnp.einsum("krj,cj->krc", source, lon_green, precision=lax.Precision.HIGHEST)
    sal = jnp.einsum(
        "rs,ksc->krc",
        lat_green,
        lax.all_gather(mixed, "lat", axis=1, tiled=True),
        precision=lax.Precision.HIGHEST,
    )
    potential = elevation - equilibrium - sal
    first_row = lax.axis_index("lat") * rows_here
    stretch, coriolis = row_terms(first_row + jnp.arange(rows_here), total_rows)
    flows = jnp.concatenate([transport_u, transport_v], axis=0)
    widened = extend(jnp.concatenate([potential, flows], axis=0), 1)
    east_slope, north_slope = slopes(widened[:12], stretch)
    flows = relax(
        widened[12:], east_slope, north_slope, ocean_depth, bottom_drag, wet_frac, coriolis
    )
    flows = relax(
        extend(flows, 1), east_slope, north_slope, ocean_depth, bottom_drag, wet_frac, coriolis
    )
    around_all = extend(flows, 1)
    east_ext = around_all[:12, 1:-1, :]
    north_ext = around_all[12:, :, 1:-1]
    elevation_next = surface(east_ext, north_ext, stretch, wet_frac)
    return (elevation_next, flows[:12], flows[12:])


def solution(mesh):
    placed = (
        P(None, "lat", "lon"),
        P(None, "lat", "lon"),
        P(None, "lat", "lon"),
        P(None, "lat", "lon"),
        P("lat", "lon"),
        P("lat", "lon"),
        P("lat", "lon"),
        P("lon", None),
        P("lat", "lon"),
    )
    return jax.shard_map(
        per_device,
        mesh=mesh,
        in_specs=placed,
        out_specs=(P(None, "lat", "lon"), P(None, "lat", "lon"), P(None, "lat", "lon")),
        check_vma=False,
    )
```

profile of v0, /device:TPU:2, one launch (start us, length us, event | category | flops | bytes accessed | tf_op | source)
XLA Modules:
  0.0 202.3 jit_solution(10215366285293022981)
XLA Ops:
  7.3 0.9 convert_element_type.21
  8.2 0.6 copy-done.13
  8.8 2.5 %fusion.20 = f32[12,96,128]{2,1,0:T(8,128)} fusion(f32[12,96,128]{2,1,0:T(8,128)} %param.12, f32[96,128]{1,0:T(8,128)S(1)} %convert_element_type.21, f32[128,128]{1,0:T(8,128)} %param.19), kind=kOutput, calls=%fused_computation.86 | convolution fusion | flops 226639872 | bytes 1294336 | tf_op jit(solution)/shard_map/krj,cj->krc/dot_general | solution.py:92
  11.3 0.6 broadcast_multiply_fusion.2
  12.0 0.7 broadcast_multiply_fusion
  12.7 0.7 broadcast_add_fusion
  13.3 67.3 %all-gather.2.cloned.1.call-done = f32[12,1536,128]{2,1,0:T(8,128)} async-done(((f32[12,96,128]{2,1,0:T(8,128)}), f32[12,1536,128]{2,1,0:T(8,128)}) %all-gather.2.cloned.1.call-update) | async-done | bytes 9437200 | tf_op jit(solution)/shard_map/all_gather | solution.py:96
  80.6 8.3 %fusion = f32[12,96,128]{2,1,0:T(8,128)S(1)} fusion(f32[12,1536,128]{2,1,0:T(8,128)} %all-gather.2.cloned.1.call-done, f32[96,1536]{1,0:T(8,128)S(1)} %copy-done, f32[12,96,128]{2,1,0:T(8,128)S(1)} %copy-done.11, f32[12,96,128]{2,1,0:T(8,128)S(1)} %copy-done.21), kind=kOutput, calls=%fused_computation.11 | convolution fusion | flops 2718203904 | bytes 11796480 | tf_op jit(solution)/shard_map/rs,ksc->krc/dot_general | solution.py:93
  89.0 0.1 pad_maximum_fusion
  89.1 1.9 fusion.56
  91.0 2.6 %copy.15 = f32[36,96,1]{1,2,0:T(1,128)} copy(f32[36,96,1]{2,1,0:T(8,128)} %get-tuple-element.26) | data formatting | bytes 27648 | tf_op jit(solution)/shard_map/slice | solution.py:17
  93.6 7.5 %collective-permute-start = (f32[36,96,1]{1,2,0:T(1,128)}, f32[36,96,1]{1,2,0:T(1,128)}, u32[]{:S(2)}, u32[]{:S(2)}) collective-permute-start(f32[36,96,1]{1,2,0:T(1,128)} %copy.15), channel_id=1, source_target_pairs={{16,0},{32,16},{48,32},{64,48},{80,64},{96,80},{112,96},{128,112},... | collective-permute-start | bytes 41480 | tf_op jit(solution)/shard_map/ppermute | solution.py:19
  101.0 1.1 copy.17
  102.2 1.9 collective-permute-start.1
  104.2 1.3 copy.16
  105.5 6.3 %collective-permute-done.1 = f32[36,96,1]{1,2,0:T(1,128)} collective-permute-done((f32[36,96,1]{1,2,0:T(1,128)}, f32[36,96,1]{1,2,0:T(1,128)}, u32[]{:S(2)}, u32[]{:S(2)}) %collective-permute-start.1) | collective-permute-done | bytes 13856 | tf_op jit(solution)/shard_map/ppermute | solution.py:18
  111.8 2.5 %copy.18 = f32[36,96,1]{2,1,0:T(8,128)} copy(f32[36,96,1]{1,2,0:T(1,128)} %collective-permute-done.1) | data formatting | bytes 27648 | tf_op jit(solution)/shard_map/ppermute | solution.py:18
  114.3 1.4 pad_maximum_fusion.47
  115.7 1.9 collective-permute-start.2
  117.7 5.8 %collective-permute-start.3 = (f32[36,1,130]{2,1,0:T(1,128)S(1)}, f32[36,1,130]{2,1,0:T(1,128)S(1)}, u32[]{:S(2)}, u32[]{:S(2)}) collective-permute-start(f32[36,1,130]{2,1,0:T(1,128)S(1)} %get-tuple-element.20), channel_id=1, source_target_pairs={{1,0},{2,1},{3,2},{4,3},{5,4},{6,5},{7,6},{8,7},{9,8},{10,9},{11,1... | collective-permute-start | bytes 56168 | tf_op jit(solution)/shard_map/ppermute | solution.py:19
  123.5 1.5 collective-permute-done.3
  125.0 2.3 %fusion.4 = f32[24,96,128]{2,1,0:T(8,128)S(1)} fusion(f32[36,96,1]{2,1,0:T(8,128)S(1)} %copy.16, f32[12,96,128]{2,1,0:T(8,128)S(1)} %copy-done.2, f32[12,96,128]{2,1,0:T(8,128)S(1)} %copy-done.4, f32[12,96,128]{2,1,0:T(8,128)S(1)} %fusion, f32[36,96,1]{2,1,0:T(8,128)S(1)} %copy-done.1, f32[36,1,130]{2,1,0:T(1,128)S(1)} %collective-permute-done.3, ...), kind=kLoop, calls=%fused_computation.32 | loop fusion | flops 5603328 | bytes 3014208 | tf_op jit(solution)/shard_map/add | solution.py:59
  127.4 1.4 fusion.16
  128.8 1.3 fusion.13
  130.2 0.5 fusion.23
  130.7 0.2 fusion.26
  131.0 0.5 copy-done.14
  131.5 0.1 maximum_multiply_fusion
  131.6 0.4 slice_maximum_fusion.1
  132.0 0.4 copy-done.8
  132.4 0.4 copy.21
  132.8 1.9 collective-permute-start.4
  134.7 0.4 copy.22
  135.1 7.5 %collective-permute-start.5 = (f32[24,96,1]{1,0,2:T(8,128)S(1)}, f32[24,96,1]{1,0,2:T(8,128)}, u32[]{:S(2)}, u32[]{:S(2)}) collective-permute-start(f32[24,96,1]{1,0,2:T(8,128)S(1)} %copy.22), channel_id=1, source_target_pairs={{16,0},{32,16},{48,32},{64,48},{80,64},{96,80},{112,96},{128,112},... | collective-permute-start | bytes 27656 | tf_op jit(solution)/shard_map/ppermute | solution.py:19
  142.7 0.4 copy.23
  143.1 1.0 collective-permute-done.5
  144.0 1.1 copy.24
  145.2 1.1 pad_maximum_fusion.55
  146.3 1.9 collective-permute-start.6
  148.2 6.1 %collective-permute-start.7 = (f32[24,1,130]{2,1,0:T(1,128)S(1)}, f32[24,1,130]{2,1,0:T(1,128)S(1)}, u32[]{:S(2)}, u32[]{:S(2)}) collective-permute-start(f32[24,1,130]{2,1,0:T(1,128)S(1)} %get-tuple-element.24), channel_id=1, source_target_pairs={{1,0},{2,1},{3,2},{4,3},{5,4},{6,5},{7,6},{8,7},{9,8},{10,9},{11,1... | collective-permute-start | bytes 37448 | tf_op jit(solution)/shard_map/ppermute | solution.py:19
  154.3 1.3 collective-permute-done.7
  155.6 1.6 fusion.1
  157.4 0.1 fusion.11
  157.5 0.6 copy-done.18
  158.1 0.6 fusion.32
  158.7 0.2 fusion.36
  159.0 0.6 copy-done.15
  159.6 0.4 pad_maximum_fusion.1
  160.0 0.4 copy-done.6
  160.4 0.4 copy.27
  160.8 7.9 %collective-permute-start.8 = (f32[24,96,1]{1,0,2:T(8,128)S(1)}, f32[24,96,1]{1,0,2:T(8,128)S(1)}, u32[]{:S(2)}, u32[]{:S(2)}) collective-permute-start(f32[24,96,1]{1,0,2:T(8,128)S(1)} %copy.27), channel_id=1, source_target_pairs={{16,0},{32,16},{48,32},{64,48},{80,64},{96,80},{112,96},{128,112},... | collective-permute-start | bytes 27656 | tf_op jit(solution)/shard_map/ppermute | solution.py:19
  168.7 0.4 copy.29
  169.1 1.9 collective-permute-start.9
  171.0 0.4 copy.28
  171.5 6.9 %collective-permute-done.9 = f32[24,96,1]{1,0,2:T(8,128)} collective-permute-done((f32[24,96,1]{1,0,2:T(8,128)S(1)}, f32[24,96,1]{1,0,2:T(8,128)}, u32[]{:S(2)}, u32[]{:S(2)}) %collective-permute-start.9) | collective-permute-done | bytes 9248 | tf_op jit(solution)/shard_map/ppermute | solution.py:18
  178.4 1.1 copy.30
  179.6 1.1 pad_maximum_fusion.51
  180.7 4.9 %collective-permute-start.10 = (f32[24,1,130]{2,1,0:T(1,128)S(1)}, f32[24,1,130]{2,1,0:T(1,128)S(1)}, u32[]{:S(2)}, u32[]{:S(2)}) collective-permute-start(f32[24,1,130]{2,1,0:T(1,128)S(1)} %get-tuple-element.21), channel_id=1, source_target_pairs={{1,0},{2,1},{3,2},{4,3},{5,4},{6,5},{7,6},{8,7},{9,8},{10,9},{11,1... | collective-permute-start | bytes 37448 | tf_op jit(solution)/shard_map/ppermute | solution.py:19
  185.6 1.9 collective-permute-start.11
  187.5 5.3 %collective-permute-done.11 = f32[24,1,130]{2,1,0:T(1,128)S(1)} collective-permute-done((f32[24,1,130]{2,1,0:T(1,128)S(1)}, f32[24,1,130]{2,1,0:T(1,128)S(1)}, u32[]{:S(2)}, u32[]{:S(2)}) %collective-permute-start.11) | collective-permute-done | bytes 12512 | tf_op jit(solution)/shard_map/ppermute | solution.py:18
  192.9 0.9 fusion.8
  193.8 0.1 fusion.39
  193.9 0.7 copy-done.16
  194.6 0.9 maximum_multiply_fusion.4
  (84 shorter events, 0.5 us)
Async XLA Ops:
  7.2 73.4 %copy-start = (f32[96,1536]{1,0:T(8,128)S(1)}, f32[96,1536]{1,0:T(8,128)}, u32[]{:S(2)}) copy-start(f32[96,1536]{1,0:T(8,128)} %param.20) | copy-start | bytes 1769476
  7.2 73.4 %copy-start.11 = (f32[12,96,128]{2,1,0:T(8,128)S(1)}, f32[12,96,128]{2,1,0:T(8,128)}, u32[]{:S(2)}) copy-start(f32[12,96,128]{2,1,0:T(8,128)} %param.12) | copy-start | bytes 1769476
  7.2 4.8 %copy-start.26 = (f32[96,128]{1,0:T(8,128)S(1)}, f32[96,128]{1,0:T(8,128)}, u32[]{:S(2)}) copy-start(f32[96,128]{1,0:T(8,128)} %param.16) | copy-start | bytes 147460
  7.2 5.4 %copy-start.27 = (f32[96,128]{1,0:T(8,128)S(1)}, f32[96,128]{1,0:T(8,128)}, u32[]{:S(2)}) copy-start(f32[96,128]{1,0:T(8,128)} %param.17) | copy-start | bytes 147460
  7.2 73.4 %copy-start.21 = (f32[12,96,128]{2,1,0:T(8,128)S(1)}, f32[12,96,128]{2,1,0:T(8,128)}, u32[]{:S(2)}) copy-start(f32[12,96,128]{2,1,0:T(8,128)} %param.13) | copy-start | bytes 1769476
  7.2 73.4 %all-gather.2.cloned.1.call-start = ((), (), s32[]{:S(2)}) async-start(), calls=%async_computation | async-start | bytes 10027008 | tf_op jit(solution)/shard_map/all_gather | solution.py:96
  8.2 0.6 copy-start.13
  12.0 118.2 %copy-start.35 = (f32[96]{0:T(128)}, f32[96]{0:T(128)S(1)}, u32[]{:S(2)}) copy-start(f32[96]{0:T(128)S(1)} %get-tuple-element.54) | copy-start | bytes 1156
  13.3 75.6 %copy-start.2 = (f32[12,96,128]{2,1,0:T(8,128)S(1)}, f32[12,96,128]{2,1,0:T(8,128)}, u32[]{:S(2)}) copy-start(f32[12,96,128]{2,1,0:T(8,128)} %param.15) | copy-start | bytes 1769476
  13.3 75.6 %copy-start.3 = (f32[12,96,128]{2,1,0:T(8,128)S(1)}, f32[12,96,128]{2,1,0:T(8,128)}, u32[]{:S(2)}) copy-start(f32[12,96,128]{2,1,0:T(8,128)} %param.14) | copy-start | bytes 1769476
  93.6 10.6 %collective-permute-start = (f32[36,96,1]{1,2,0:T(1,128)}, f32[36,96,1]{1,2,0:T(1,128)}, u32[]{:S(2)}, u32[]{:S(2)}) collective-permute-start(f32[36,96,1]{1,2,0:T(1,128)} %copy.15), channel_id=1, source_target_pairs={{16,0},{32,16},{48,32},{64,48},{80,64},{96,80},{112,96},{128,112},... | collective-permute-start | bytes 41480 | tf_op jit(solution)/shard_map/ppermute | solution.py:19
  102.2 9.6 %collective-permute-start.1 = (f32[36,96,1]{1,2,0:T(1,128)}, f32[36,96,1]{1,2,0:T(1,128)}, u32[]{:S(2)}, u32[]{:S(2)}) collective-permute-start(f32[36,96,1]{1,2,0:T(1,128)} %copy.17), channel_id=1, source_target_pairs={{0,16},{16,32},{32,48},{48,64},{64,80},{80,96},{96,112},{112,128},... | collective-permute-start | bytes 41480 | tf_op jit(solution)/shard_map/ppermute | solution.py:18
  104.2 23.2 %copy-start.33 = (f32[96]{0:T(128)}, f32[96]{0:T(128)S(1)}, u32[]{:S(2)}) copy-start(f32[96]{0:T(128)S(1)} %divide_multiply_fusion) | copy-start | bytes 1156
  114.3 10.7 %copy-start.1 = (f32[36,96,1]{2,1,0:T(8,128)S(1)}, f32[36,96,1]{2,1,0:T(8,128)}, u32[]{:S(2)}) copy-start(f32[36,96,1]{2,1,0:T(8,128)} %copy.18) | copy-start | bytes 41476
  114.3 10.7 %copy-start.4 = (f32[12,96,128]{2,1,0:T(8,128)S(1)}, f32[12,96,128]{2,1,0:T(8,128)}, u32[]{:S(2)}) copy-start(f32[12,96,128]{2,1,0:T(8,128)} %param.14) | copy-start | bytes 1769476
  115.7 7.8 %collective-permute-start.2 = (f32[36,1,130]{2,1,0:T(1,128)S(1)}, f32[36,1,130]{2,1,0:T(1,128)S(1)}, u32[]{:S(2)}, u32[]{:S(2)}) collective-permute-start(f32[36,1,130]{2,1,0:T(1,128)S(1)} %get-tuple-element.19), channel_id=1, source_target_pairs={{0,1},{1,2},{2,3},{3,4},{4,5},{5,6},{6,7},{7,8},{8,9},{9,10},{10,1... | collective-permute-start | bytes 56168 | tf_op jit(solution)/shard_map/ppermute | solution.py:18
  117.7 7.4 %collective-permute-start.3 = (f32[36,1,130]{2,1,0:T(1,128)S(1)}, f32[36,1,130]{2,1,0:T(1,128)S(1)}, u32[]{:S(2)}, u32[]{:S(2)}) collective-permute-start(f32[36,1,130]{2,1,0:T(1,128)S(1)} %get-tuple-element.20), channel_id=1, source_target_pairs={{1,0},{2,1},{3,2},{4,3},{5,4},{6,5},{7,6},{8,7},{9,8},{10,9},{11,1... | collective-permute-start | bytes 56168 | tf_op jit(solution)/shard_map/ppermute | solution.py:19
  123.5 7.3 %copy-start.31 = (f32[96]{0:T(128)}, f32[96]{0:T(128)S(1)}, u32[]{:S(2)}) copy-start(f32[96]{0:T(128)S(1)} %fusion.52) | copy-start | bytes 1156
  123.5 3.9 %copy-start.25 = (f32[96,128]{1,0:T(8,128)S(1)}, f32[96,128]{1,0:T(8,128)}, u32[]{:S(2)}) copy-start(f32[96,128]{1,0:T(8,128)} %get-tuple-element.53) | copy-start | bytes 147460
  127.4 1.4 copy-start.24
  128.8 1.4 copy-start.17
  128.8 1.4 copy-start.19
  128.8 1.4 copy-start.22
  128.8 1.4 copy-start.28
  128.8 1.4 copy-start.29
  128.8 1.4 copy-start.37
  130.7 0.8 copy-start.14
  131.6 0.8 copy-start.8
  132.8 9.9 %collective-permute-start.4 = (f32[24,96,1]{1,0,2:T(8,128)S(1)}, f32[24,96,1]{1,0,2:T(8,128)S(1)}, u32[]{:S(2)}, u32[]{:S(2)}) collective-permute-start(f32[24,96,1]{1,0,2:T(8,128)S(1)} %copy.21), channel_id=1, source_target_pairs={{0,16},{16,32},{32,48},{48,64},{64,80},{80,96},{96,112},{112,128},... | collective-permute-start | bytes 27656 | tf_op jit(solution)/shard_map/ppermute | solution.py:18
  135.1 8.9 %collective-permute-start.5 = (f32[24,96,1]{1,0,2:T(8,128)S(1)}, f32[24,96,1]{1,0,2:T(8,128)}, u32[]{:S(2)}, u32[]{:S(2)}) collective-permute-start(f32[24,96,1]{1,0,2:T(8,128)S(1)} %copy.22), channel_id=1, source_target_pairs={{16,0},{32,16},{48,32},{64,48},{80,64},{96,80},{112,96},{128,112},... | collective-permute-start | bytes 27656 | tf_op jit(solution)/shard_map/ppermute | solution.py:19
  145.2 10.5 %copy-start.9 = (f32[12,96,128]{2,1,0:T(8,128)S(1)}, f32[12,96,128]{2,1,0:T(8,128)}, u32[]{:S(2)}) copy-start(f32[12,96,128]{2,1,0:T(8,128)} %copy-done.8) | copy-start | bytes 1769476
  146.3 8.0 %collective-permute-start.6 = (f32[24,1,130]{2,1,0:T(1,128)S(1)}, f32[24,1,130]{2,1,0:T(1,128)S(1)}, u32[]{:S(2)}, u32[]{:S(2)}) collective-permute-start(f32[24,1,130]{2,1,0:T(1,128)S(1)} %get-tuple-element.23), channel_id=1, source_target_pairs={{0,1},{1,2},{2,3},{3,4},{4,5},{5,6},{6,7},{7,8},{8,9},{9,10},{10,1... | collective-permute-start | bytes 37448 | tf_op jit(solution)/shard_map/ppermute | solution.py:18
  148.2 9.1 %copy-start.10 = (f32[12,96,128]{2,1,0:T(8,128)S(1)}, f32[12,96,128]{2,1,0:T(8,128)}, u32[]{:S(2)}) copy-start(f32[12,96,128]{2,1,0:T(8,128)} %get-tuple-element.16) | copy-start | bytes 1769476
  148.2 9.1 %copy-start.12 = (f32[12,96,128]{2,1,0:T(8,128)S(1)}, f32[12,96,128]{2,1,0:T(8,128)}, u32[]{:S(2)}) copy-start(f32[12,96,128]{2,1,0:T(8,128)} %get-tuple-element.18) | copy-start | bytes 1769476
  148.2 7.4 %collective-permute-start.7 = (f32[24,1,130]{2,1,0:T(1,128)S(1)}, f32[24,1,130]{2,1,0:T(1,128)S(1)}, u32[]{:S(2)}, u32[]{:S(2)}) collective-permute-start(f32[24,1,130]{2,1,0:T(1,128)S(1)} %get-tuple-element.24), channel_id=1, source_target_pairs={{1,0},{2,1},{3,2},{4,3},{5,4},{6,5},{7,6},{8,7},{9,8},{10,9},{11,1... | collective-permute-start | bytes 37448 | tf_op jit(solution)/shard_map/ppermute | solution.py:19
  157.3 0.8 copy-start.18
  157.3 0.8 copy-start.20
  157.3 0.8 copy-start.23
  157.3 0.8 copy-start.30
  157.3 0.8 copy-start.32
  157.3 0.8 copy-start.36
  157.3 0.8 copy-start.38
  158.7 0.8 copy-start.15
  159.6 0.8 copy-start.6
  159.6 33.3 %copy-start.5 = (f32[12,96,128]{2,1,0:T(8,128)}, f32[12,96,128]{2,1,0:T(8,128)S(1)}, u32[]{:S(2)}) copy-start(f32[12,96,128]{2,1,0:T(8,128)S(1)} %get-tuple-element.45) | copy-start | bytes 1769476
  160.8 10.2 %collective-permute-start.8 = (f32[24,96,1]{1,0,2:T(8,128)S(1)}, f32[24,96,1]{1,0,2:T(8,128)S(1)}, u32[]{:S(2)}, u32[]{:S(2)}) collective-permute-start(f32[24,96,1]{1,0,2:T(8,128)S(1)} %copy.27), channel_id=1, source_target_pairs={{16,0},{32,16},{48,32},{64,48},{80,64},{96,80},{112,96},{128,112},... | collective-permute-start | bytes 27656 | tf_op jit(solution)/shard_map/ppermute | solution.py:19
  169.1 9.3 %collective-permute-start.9 = (f32[24,96,1]{1,0,2:T(8,128)S(1)}, f32[24,96,1]{1,0,2:T(8,128)}, u32[]{:S(2)}, u32[]{:S(2)}) collective-permute-start(f32[24,96,1]{1,0,2:T(8,128)S(1)} %copy.29), channel_id=1, source_target_pairs={{0,16},{16,32},{32,48},{48,64},{64,80},{80,96},{96,112},{112,128},... | collective-permute-start | bytes 27656 | tf_op jit(solution)/shard_map/ppermute | solution.py:18
  179.5 13.3 %copy-start.7 = (f32[12,96,128]{2,1,0:T(8,128)S(1)}, f32[12,96,128]{2,1,0:T(8,128)}, u32[]{:S(2)}) copy-start(f32[12,96,128]{2,1,0:T(8,128)} %copy-done.6) | copy-start | bytes 1769476
  179.5 13.3 %copy-start.34 = (f32[96]{0:T(128)S(1)}, f32[96]{0:T(128)}, u32[]{:S(2)}) copy-start(f32[96]{0:T(128)} %copy-done.33) | copy-start | bytes 1156
  180.7 6.9 %collective-permute-start.10 = (f32[24,1,130]{2,1,0:T(1,128)S(1)}, f32[24,1,130]{2,1,0:T(1,128)S(1)}, u32[]{:S(2)}, u32[]{:S(2)}) collective-permute-start(f32[24,1,130]{2,1,0:T(1,128)S(1)} %get-tuple-element.21), channel_id=1, source_target_pairs={{1,0},{2,1},{3,2},{4,3},{5,4},{6,5},{7,6},{8,7},{9,8},{10,9},{11,1... | collective-permute-start | bytes 37448 | tf_op jit(solution)/shard_map/ppermute | solution.py:19
  185.6 8.2 %copy-start.39 = (f32[6]{0:T(128)S(1)}, f32[6]{0:T(128)}, u32[]{:S(2)}) copy-start(f32[6]{0:T(128)} %constant.32) | copy-start | bytes 76
  185.6 7.3 %collective-permute-start.11 = (f32[24,1,130]{2,1,0:T(1,128)S(1)}, f32[24,1,130]{2,1,0:T(1,128)S(1)}, u32[]{:S(2)}, u32[]{:S(2)}) collective-permute-start(f32[24,1,130]{2,1,0:T(1,128)S(1)} %get-tuple-element.22), channel_id=1, source_target_pairs={{0,1},{1,2},{2,3},{3,4},{4,5},{5,6},{6,7},{7,8},{8,9},{9,10},{10,1... | collective-permute-start | bytes 37448 | tf_op jit(solution)/shard_map/ppermute | solution.py:18
  193.8 0.8 copy-start.16
Sparse Core Ops, SparseCore 0:
  11.5 69.0 all-gather.1
where the time goes:
time: 203 us; the launch traced here: 202 us
  waiting for transfers between devices  89.7 us (44%)
  starting transfers between devices  51.2 us (25%)
  local copies, waits for them, and re-layouts  17.9 us (9%)
  other arithmetic  17.9 us (9%)
  between operations  14.7 us (7%)
  matrix products  10.9 us (5%)
    all_gather x1, waiting for transfers between devices, per_device(): lax.all_gather(mixed, 'lat', axis=1, tiled=True)  67.3 us
    ppermute x6, starting transfers between devices, extended(): after = lax.ppermute(initial, axis, down)  39.7 us
    ppermute x6, waiting for transfers between devices, extended(): before = lax.ppermute(last, axis, up)  18.6 us
    ppermute x6, starting transfers between devices, extended(): before = lax.ppermute(last, axis, up)  11.5 us
    dot_general x1, matrix products, per_device(): jnp.einsum('rs,ksc->krc', lat_green, lax.all_gather(mixed, 'lat', axis=1,...  8.35 us
  transfers between devices with their start and end apart: 13, of which 7 were waited for; matrix products, arithmetic and copies ran while one was open for 3% of the time, Pallas kernels for 0%

commit v1 on v0

--- a/solution.py
+++ b/solution.py
@@ -93,7 +93,9 @@
     sal = jnp.einsum(
         "rs,ksc->krc",
         lat_green,
-        lax.all_gather(mixed, "lat", axis=1, tiled=True),
+        jnp.concatenate(
+            lax.all_to_all(jnp.stack([mixed] * lax.axis_size("lat")), "lat", 0, 0), axis=1
+        ),
         precision=lax.Precision.HIGHEST,
     )
     potential = elevation - equilibrium - sal

time: 203 us -> 281 us (1.38)
  waiting for transfers between devices: 89.7 us -> 159 us
  starting transfers between devices: 51.2 us -> 67.4 us
  between operations: 14.7 us -> 1.31 us
  local copies, waits for them, and re-layouts: 17.9 us -> 27.4 us
  matrix products: 10.9 us -> 7.54 us
    all_to_all x0 -> x1, waiting for transfers between devices: none -> 136 us  [per_device(): lax.all_to_all(jnp.stack([mixed] * lax.axis_size('lat')), 'lat', 0, 0)]
    all_gather x1 -> x0, waiting for transfers between devices: 67.3 us -> none  [per_device(): lax.all_gather(mixed, 'lat', axis=1, tiled=True)]
    all_to_all x0 -> x1, starting transfers between devices: none -> 10.6 us  [per_device(): lax.all_to_all(jnp.stack([mixed] * lax.axis_size('lat')), 'lat', 0, 0)]
    ppermute x6, starting transfers between devices: 39.7 us -> 45.3 us  [extended(): after = lax.ppermute(initial, axis, down)]
    another operation x0 -> x1, local copies, waits for them, and re-layouts: none -> 4.79 us  [per_device(): jnp.stack([mixed] * lax.axis_size('lat'))]
    reshape x0 -> x1, local copies, waits for them, and re-layouts: none -> 4.62 us  [per_device(): jnp.concatenate(lax.all_to_all(jnp.stack([mixed] * lax.axis_size('lat')),...]
  transfers between devices with their start and end apart: 13 -> 13, of which waited for: 7 -> 7; matrix products, arithmetic and copies ran while one was open for 3% -> 2% of each run, Pallas kernels for 0% -> 0%
where the time goes in v1:
time: 281 us; the launch traced here: 280 us
  waiting for transfers between devices  159 us (57%)
  starting transfers between devices  67.4 us (24%)
  local copies, waits for them, and re-layouts  27.4 us (10%)
  other arithmetic  17.8 us (6%)
  matrix products  7.54 us (3%)
    all_to_all x1, waiting for transfers between devices, per_device(): lax.all_to_all(jnp.stack([mixed] * lax.axis_size('lat')), 'lat', 0, 0)  136 us
    ppermute x6, starting transfers between devices, extended(): after = lax.ppermute(initial, axis, down)  45.3 us
    ppermute x6, waiting for transfers between devices, extended(): before = lax.ppermute(last, axis, up)  18.6 us
    ppermute x6, starting transfers between devices, extended(): before = lax.ppermute(last, axis, up)  11.5 us
    all_to_all x1, starting transfers between devices, per_device(): lax.all_to_all(jnp.stack([mixed] * lax.axis_size('lat')), 'lat', 0, 0)  10.6 us
    dot_general x1, matrix products, per_device(): jnp.einsum('rs,ksc->krc', lat_green, jnp.concatenate(lax.all_to_all(jnp.s...  5.84 us
  transfers between devices with their start and end apart: 13, of which 7 were waited for; matrix products, arithmetic and copies ran while one was open for 2% of the time, Pallas kernels for 0%

profile of v1, /device:TPU:2, one launch (start us, length us, event | category | flops | bytes accessed | tf_op | source)
XLA Modules:
  0.0 280.1 jit_solution(6858664172806704771)
XLA Ops:
  0.6 0.9 convert_element_type.21
  1.5 0.6 copy-done.13
  2.1 1.7 fusion.20
  3.8 4.8 %stack.2 = f32[16,12,96,128]{3,2,1,0:T(8,128)} broadcast(f32[12,96,128]{2,1,0:T(8,128)S(1)} %fusion.20), dimensions={1,2,3} | broadcast | bytes 10027008 | tf_op jit(solution)/shard_map/stack | solution.py:97
  8.6 10.6 %all-to-all-start = ((f32[16,12,96,128]{3,2,1,0:T(8,128)}), f32[16,12,96,128]{3,2,1,0:T(8,128)}, u32[]{:S(2)}, u32[]{:S(2)}) async-start(f32[16,12,96,128]{3,2,1,0:T(8,128)} %stack.2), calls=%async_computation | async-start | bytes 18874368 | tf_op jit(solution)/shard_map/all_to_all | solution.py:97
  19.3 0.6 broadcast_multiply_fusion.2
  19.8 0.6 broadcast_multiply_fusion
  20.5 0.7 broadcast_add_fusion
  21.2 136.3 %all-to-all-done = f32[16,12,96,128]{3,2,1,0:T(8,128)} async-done(((f32[16,12,96,128]{3,2,1,0:T(8,128)}), f32[16,12,96,128]{3,2,1,0:T(8,128)}, u32[]{:S(2)}, u32[]{:S(2)}) %all-to-all-start) | async-done | bytes 9437216 | tf_op jit(solution)/shard_map/all_to_all | solution.py:97
  157.5 4.6 %copy.15 = f32[12,16,96,128]{3,2,1,0:T(8,128)S(1)} copy(f32[12,16,96,128]{3,2,0,1:T(8,128)} %bitcast.1) | data formatting | bytes 18874368 | tf_op jit(solution)/shard_map/reshape | solution.py:96
  162.1 5.8 %fusion = f32[12,96,128]{2,1,0:T(8,128)S(1)} fusion(f32[12,1536,128]{2,1,0:T(8,128)S(1)} %bitcast.13, f32[96,1536]{1,0:T(8,128)S(1)} %copy-done, f32[12,96,128]{2,1,0:T(8,128)S(1)} %copy-done.11, f32[12,96,128]{2,1,0:T(8,128)S(1)} %copy-done.21), kind=kOutput, calls=%fused_computation.11 | convolution fusion | flops 2718203904 | bytes 11796480 | tf_op jit(solution)/shard_map/rs,ksc->krc/dot_general | solution.py:93
  168.1 1.9 fusion.56
  170.0 2.6 copy.16
  172.6 8.4 %collective-permute-start = (f32[36,96,1]{1,2,0:T(1,128)}, f32[36,96,1]{1,2,0:T(1,128)}, u32[]{:S(2)}, u32[]{:S(2)}) collective-permute-start(f32[36,96,1]{1,2,0:T(1,128)} %copy.16), channel_id=1, source_target_pairs={{16,0},{32,16},{48,32},{64,48},{80,64},{96,80},{112,96},{128,112},... | collective-permute-start | bytes 41480 | tf_op jit(solution)/shard_map/ppermute | solution.py:19
  181.0 1.2 copy.18
  182.2 1.9 collective-permute-start.1
  184.2 1.3 copy.17
  185.5 6.3 %collective-permute-done.1 = f32[36,96,1]{1,2,0:T(1,128)} collective-permute-done((f32[36,96,1]{1,2,0:T(1,128)}, f32[36,96,1]{1,2,0:T(1,128)}, u32[]{:S(2)}, u32[]{:S(2)}) %collective-permute-start.1) | collective-permute-done | bytes 13856 | tf_op jit(solution)/shard_map/ppermute | solution.py:18
  191.8 2.5 copy.19
  194.3 1.4 pad_maximum_fusion.47
  195.7 1.9 collective-permute-start.2
  197.7 10.6 %collective-permute-start.3 = (f32[36,1,130]{2,1,0:T(1,128)S(1)}, f32[36,1,130]{2,1,0:T(1,128)S(1)}, u32[]{:S(2)}, u32[]{:S(2)}) collective-permute-start(f32[36,1,130]{2,1,0:T(1,128)S(1)} %get-tuple-element.20), channel_id=1, source_target_pairs={{1,0},{2,1},{3,2},{4,3},{5,4},{6,5},{7,6},{8,7},{9,8},{10,9},{11,1... | collective-permute-start | bytes 56168 | tf_op jit(solution)/shard_map/ppermute | solution.py:19
  208.4 1.4 collective-permute-done.3
  209.7 2.3 fusion.4
  212.1 1.4 fusion.16
  213.5 1.3 fusion.13
  214.9 0.5 fusion.23
  215.4 0.2 fusion.26
  215.7 0.5 copy-done.14
  216.3 0.4 slice_maximum_fusion.1
  216.7 0.4 copy-done.8
  217.1 0.4 copy.22
  217.5 1.9 collective-permute-start.4
  219.4 0.4 copy.23
  219.8 7.5 %collective-permute-start.5 = (f32[24,96,1]{1,0,2:T(8,128)S(1)}, f32[24,96,1]{1,0,2:T(8,128)}, u32[]{:S(2)}, u32[]{:S(2)}) collective-permute-start(f32[24,96,1]{1,0,2:T(8,128)S(1)} %copy.23), channel_id=1, source_target_pairs={{16,0},{32,16},{48,32},{64,48},{80,64},{96,80},{112,96},{128,112},... | collective-permute-start | bytes 27656 | tf_op jit(solution)/shard_map/ppermute | solution.py:19
  227.4 0.4 copy.24
  227.8 1.0 collective-permute-done.5
  228.7 1.1 copy.25
  229.9 1.1 pad_maximum_fusion.55
  231.0 1.9 collective-permute-start.6
  232.9 5.9 %collective-permute-start.7 = (f32[24,1,130]{2,1,0:T(1,128)S(1)}, f32[24,1,130]{2,1,0:T(1,128)S(1)}, u32[]{:S(2)}, u32[]{:S(2)}) collective-permute-start(f32[24,1,130]{2,1,0:T(1,128)S(1)} %get-tuple-element.24), channel_id=1, source_target_pairs={{1,0},{2,1},{3,2},{4,3},{5,4},{6,5},{7,6},{8,7},{9,8},{10,9},{11,1... | collective-permute-start | bytes 37448 | tf_op jit(solution)/shard_map/ppermute | solution.py:19
  238.8 1.5 collective-permute-done.7
  240.3 1.6 fusion.1
  242.1 0.1 fusion.11
  242.2 0.6 copy-done.18
  242.8 0.6 fusion.32
  243.4 0.2 fusion.36
  243.7 0.6 copy-done.15
  244.3 0.4 pad_maximum_fusion.1
  244.7 0.4 copy-done.6
  245.1 0.4 copy.28
  245.5 7.9 %collective-permute-start.8 = (f32[24,96,1]{1,0,2:T(8,128)S(1)}, f32[24,96,1]{1,0,2:T(8,128)S(1)}, u32[]{:S(2)}, u32[]{:S(2)}) collective-permute-start(f32[24,96,1]{1,0,2:T(8,128)S(1)} %copy.28), channel_id=1, source_target_pairs={{16,0},{32,16},{48,32},{64,48},{80,64},{96,80},{112,96},{128,112},... | collective-permute-start | bytes 27656 | tf_op jit(solution)/shard_map/ppermute | solution.py:19
  253.4 0.4 copy.30
  253.8 1.9 collective-permute-start.9
  255.7 0.4 copy.29
  256.2 6.9 %collective-permute-done.9 = f32[24,96,1]{1,0,2:T(8,128)} collective-permute-done((f32[24,96,1]{1,0,2:T(8,128)S(1)}, f32[24,96,1]{1,0,2:T(8,128)}, u32[]{:S(2)}, u32[]{:S(2)}) %collective-permute-start.9) | collective-permute-done | bytes 9248 | tf_op jit(solution)/shard_map/ppermute | solution.py:18
  263.1 1.1 copy.31
  264.3 1.1 pad_maximum_fusion.51
  265.4 4.9 %collective-permute-start.10 = (f32[24,1,130]{2,1,0:T(1,128)S(1)}, f32[24,1,130]{2,1,0:T(1,128)S(1)}, u32[]{:S(2)}, u32[]{:S(2)}) collective-permute-start(f32[24,1,130]{2,1,0:T(1,128)S(1)} %get-tuple-element.21), channel_id=1, source_target_pairs={{1,0},{2,1},{3,2},{4,3},{5,4},{6,5},{7,6},{8,7},{9,8},{10,9},{11,1... | collective-permute-start | bytes 37448 | tf_op jit(solution)/shard_map/ppermute | solution.py:19
  270.3 1.9 collective-permute-start.11
  272.2 5.3 %collective-permute-done.11 = f32[24,1,130]{2,1,0:T(1,128)S(1)} collective-permute-done((f32[24,1,130]{2,1,0:T(1,128)S(1)}, f32[24,1,130]{2,1,0:T(1,128)S(1)}, u32[]{:S(2)}, u32[]{:S(2)}) %collective-permute-start.11) | collective-permute-done | bytes 12512 | tf_op jit(solution)/shard_map/ppermute | solution.py:18
  277.6 0.9 fusion.8
  278.6 0.7 copy-done.16
  279.3 0.9 maximum_multiply_fusion.4
  (85 shorter events, 0.7 us)
Async XLA Ops:
  0.6 161.5 %copy-start = (f32[96,1536]{1,0:T(8,128)S(1)}, f32[96,1536]{1,0:T(8,128)}, u32[]{:S(2)}) copy-start(f32[96,1536]{1,0:T(8,128)} %param.20) | copy-start | bytes 1769476
  1.5 0.6 copy-start.13
  8.6 11.2 %copy-start.26 = (f32[96,128]{1,0:T(8,128)S(1)}, f32[96,128]{1,0:T(8,128)}, u32[]{:S(2)}) copy-start(f32[96,128]{1,0:T(8,128)} %param.16) | copy-start | bytes 147460
  8.6 11.9 %copy-start.27 = (f32[96,128]{1,0:T(8,128)S(1)}, f32[96,128]{1,0:T(8,128)}, u32[]{:S(2)}) copy-start(f32[96,128]{1,0:T(8,128)} %param.17) | copy-start | bytes 147460
  8.6 148.8 %all-to-all-start = ((f32[16,12,96,128]{3,2,1,0:T(8,128)}), f32[16,12,96,128]{3,2,1,0:T(8,128)}, u32[]{:S(2)}, u32[]{:S(2)}) async-start(f32[16,12,96,128]{3,2,1,0:T(8,128)} %stack.2), calls=%async_computation | async-start | bytes 18874368 | tf_op jit(solution)/shard_map/all_to_all | solution.py:97
  19.8 195.0 %copy-start.35 = (f32[96]{0:T(128)}, f32[96]{0:T(128)S(1)}, u32[]{:S(2)}) copy-start(f32[96]{0:T(128)S(1)} %get-tuple-element.54) | copy-start | bytes 1156
  157.5 4.6 %copy-start.11 = (f32[12,96,128]{2,1,0:T(8,128)S(1)}, f32[12,96,128]{2,1,0:T(8,128)}, u32[]{:S(2)}) copy-start(f32[12,96,128]{2,1,0:T(8,128)} %param.12) | copy-start | bytes 1769476
  157.5 4.7 %copy-start.21 = (f32[12,96,128]{2,1,0:T(8,128)S(1)}, f32[12,96,128]{2,1,0:T(8,128)}, u32[]{:S(2)}) copy-start(f32[12,96,128]{2,1,0:T(8,128)} %param.13) | copy-start | bytes 1769476
  162.1 5.9 %copy-start.2 = (f32[12,96,128]{2,1,0:T(8,128)S(1)}, f32[12,96,128]{2,1,0:T(8,128)}, u32[]{:S(2)}) copy-start(f32[12,96,128]{2,1,0:T(8,128)} %param.15) | copy-start | bytes 1769476
  162.1 5.9 %copy-start.3 = (f32[12,96,128]{2,1,0:T(8,128)S(1)}, f32[12,96,128]{2,1,0:T(8,128)}, u32[]{:S(2)}) copy-start(f32[12,96,128]{2,1,0:T(8,128)} %param.14) | copy-start | bytes 1769476
  172.6 11.5 %collective-permute-start = (f32[36,96,1]{1,2,0:T(1,128)}, f32[36,96,1]{1,2,0:T(1,128)}, u32[]{:S(2)}, u32[]{:S(2)}) collective-permute-start(f32[36,96,1]{1,2,0:T(1,128)} %copy.16), channel_id=1, source_target_pairs={{16,0},{32,16},{48,32},{64,48},{80,64},{96,80},{112,96},{128,112},... | collective-permute-start | bytes 41480 | tf_op jit(solution)/shard_map/ppermute | solution.py:19
  182.2 9.6 %collective-permute-start.1 = (f32[36,96,1]{1,2,0:T(1,128)}, f32[36,96,1]{1,2,0:T(1,128)}, u32[]{:S(2)}, u32[]{:S(2)}) collective-permute-start(f32[36,96,1]{1,2,0:T(1,128)} %copy.18), channel_id=1, source_target_pairs={{0,16},{16,32},{32,48},{48,64},{64,80},{80,96},{96,112},{112,128},... | collective-permute-start | bytes 41480 | tf_op jit(solution)/shard_map/ppermute | solution.py:18
  184.2 27.9 %copy-start.33 = (f32[96]{0:T(128)}, f32[96]{0:T(128)S(1)}, u32[]{:S(2)}) copy-start(f32[96]{0:T(128)S(1)} %divide_multiply_fusion) | copy-start | bytes 1156
  194.3 15.4 %copy-start.1 = (f32[36,96,1]{2,1,0:T(8,128)S(1)}, f32[36,96,1]{2,1,0:T(8,128)}, u32[]{:S(2)}) copy-start(f32[36,96,1]{2,1,0:T(8,128)} %copy.19) | copy-start | bytes 41476
  194.3 15.4 %copy-start.4 = (f32[12,96,128]{2,1,0:T(8,128)S(1)}, f32[12,96,128]{2,1,0:T(8,128)}, u32[]{:S(2)}) copy-start(f32[12,96,128]{2,1,0:T(8,128)} %param.14) | copy-start | bytes 1769476
  195.7 12.6 %collective-permute-start.2 = (f32[36,1,130]{2,1,0:T(1,128)S(1)}, f32[36,1,130]{2,1,0:T(1,128)S(1)}, u32[]{:S(2)}, u32[]{:S(2)}) collective-permute-start(f32[36,1,130]{2,1,0:T(1,128)S(1)} %get-tuple-element.19), channel_id=1, source_target_pairs={{0,1},{1,2},{2,3},{3,4},{4,5},{5,6},{6,7},{7,8},{8,9},{9,10},{10,1... | collective-permute-start | bytes 56168 | tf_op jit(solution)/shard_map/ppermute | solution.py:18
  197.7 12.1 %collective-permute-start.3 = (f32[36,1,130]{2,1,0:T(1,128)S(1)}, f32[36,1,130]{2,1,0:T(1,128)S(1)}, u32[]{:S(2)}, u32[]{:S(2)}) collective-permute-start(f32[36,1,130]{2,1,0:T(1,128)S(1)} %get-tuple-element.20), channel_id=1, source_target_pairs={{1,0},{2,1},{3,2},{4,3},{5,4},{6,5},{7,6},{8,7},{9,8},{10,9},{11,1... | collective-permute-start | bytes 56168 | tf_op jit(solution)/shard_map/ppermute | solution.py:19
  208.3 7.1 %copy-start.31 = (f32[96]{0:T(128)}, f32[96]{0:T(128)S(1)}, u32[]{:S(2)}) copy-start(f32[96]{0:T(128)S(1)} %fusion.52) | copy-start | bytes 1156
  208.4 3.7 %copy-start.25 = (f32[96,128]{1,0:T(8,128)S(1)}, f32[96,128]{1,0:T(8,128)}, u32[]{:S(2)}) copy-start(f32[96,128]{1,0:T(8,128)} %get-tuple-element.53) | copy-start | bytes 147460
  212.1 1.4 copy-start.24
  213.5 1.4 copy-start.17
  213.5 1.4 copy-start.19
  213.5 1.4 copy-start.22
  213.5 1.4 copy-start.28
  213.5 1.4 copy-start.29
  213.5 1.4 copy-start.37
  215.4 0.8 copy-start.14
  216.3 0.8 copy-start.8
  217.5 9.9 %collective-permute-start.4 = (f32[24,96,1]{1,0,2:T(8,128)S(1)}, f32[24,96,1]{1,0,2:T(8,128)S(1)}, u32[]{:S(2)}, u32[]{:S(2)}) collective-permute-start(f32[24,96,1]{1,0,2:T(8,128)S(1)} %copy.22), channel_id=1, source_target_pairs={{0,16},{16,32},{32,48},{48,64},{64,80},{80,96},{96,112},{112,128},... | collective-permute-start | bytes 27656 | tf_op jit(solution)/shard_map/ppermute | solution.py:18
  219.8 8.9 %collective-permute-start.5 = (f32[24,96,1]{1,0,2:T(8,128)S(1)}, f32[24,96,1]{1,0,2:T(8,128)}, u32[]{:S(2)}, u32[]{:S(2)}) collective-permute-start(f32[24,96,1]{1,0,2:T(8,128)S(1)} %copy.23), channel_id=1, source_target_pairs={{16,0},{32,16},{48,32},{64,48},{80,64},{96,80},{112,96},{128,112},... | collective-permute-start | bytes 27656 | tf_op jit(solution)/shard_map/ppermute | solution.py:19
  229.9 10.5 %copy-start.9 = (f32[12,96,128]{2,1,0:T(8,128)S(1)}, f32[12,96,128]{2,1,0:T(8,128)}, u32[]{:S(2)}) copy-start(f32[12,96,128]{2,1,0:T(8,128)} %copy-done.8) | copy-start | bytes 1769476
  231.0 7.8 %collective-permute-start.6 = (f32[24,1,130]{2,1,0:T(1,128)S(1)}, f32[24,1,130]{2,1,0:T(1,128)S(1)}, u32[]{:S(2)}, u32[]{:S(2)}) collective-permute-start(f32[24,1,130]{2,1,0:T(1,128)S(1)} %get-tuple-element.23), channel_id=1, source_target_pairs={{0,1},{1,2},{2,3},{3,4},{4,5},{5,6},{6,7},{7,8},{8,9},{9,10},{10,1... | collective-permute-start | bytes 37448 | tf_op jit(solution)/shard_map/ppermute | solution.py:18
  232.9 9.1 %copy-start.10 = (f32[12,96,128]{2,1,0:T(8,128)S(1)}, f32[12,96,128]{2,1,0:T(8,128)}, u32[]{:S(2)}) copy-start(f32[12,96,128]{2,1,0:T(8,128)} %get-tuple-element.16) | copy-start | bytes 1769476
  232.9 9.1 %copy-start.12 = (f32[12,96,128]{2,1,0:T(8,128)S(1)}, f32[12,96,128]{2,1,0:T(8,128)}, u32[]{:S(2)}) copy-start(f32[12,96,128]{2,1,0:T(8,128)} %get-tuple-element.18) | copy-start | bytes 1769476
  232.9 7.4 %collective-permute-start.7 = (f32[24,1,130]{2,1,0:T(1,128)S(1)}, f32[24,1,130]{2,1,0:T(1,128)S(1)}, u32[]{:S(2)}, u32[]{:S(2)}) collective-permute-start(f32[24,1,130]{2,1,0:T(1,128)S(1)} %get-tuple-element.24), channel_id=1, source_target_pairs={{1,0},{2,1},{3,2},{4,3},{5,4},{6,5},{7,6},{8,7},{9,8},{10,9},{11,1... | collective-permute-start | bytes 37448 | tf_op jit(solution)/shard_map/ppermute | solution.py:19
  242.0 0.8 copy-start.18
  242.0 0.8 copy-start.20
  242.0 0.8 copy-start.23
  242.0 0.8 copy-start.30
  242.0 0.8 copy-start.32
  242.0 0.8 copy-start.36
  242.0 0.8 copy-start.38
  243.4 0.8 copy-start.15
  244.3 0.8 copy-start.6
  244.3 33.3 %copy-start.5 = (f32[12,96,128]{2,1,0:T(8,128)}, f32[12,96,128]{2,1,0:T(8,128)S(1)}, u32[]{:S(2)}) copy-start(f32[12,96,128]{2,1,0:T(8,128)S(1)} %get-tuple-element.45) | copy-start | bytes 1769476
  245.5 10.2 %collective-permute-start.8 = (f32[24,96,1]{1,0,2:T(8,128)S(1)}, f32[24,96,1]{1,0,2:T(8,128)S(1)}, u32[]{:S(2)}, u32[]{:S(2)}) collective-permute-start(f32[24,96,1]{1,0,2:T(8,128)S(1)} %copy.28), channel_id=1, source_target_pairs={{16,0},{32,16},{48,32},{64,48},{80,64},{96,80},{112,96},{128,112},... | collective-permute-start | bytes 27656 | tf_op jit(solution)/shard_map/ppermute | solution.py:19
  253.8 9.3 %collective-permute-start.9 = (f32[24,96,1]{1,0,2:T(8,128)S(1)}, f32[24,96,1]{1,0,2:T(8,128)}, u32[]{:S(2)}, u32[]{:S(2)}) collective-permute-start(f32[24,96,1]{1,0,2:T(8,128)S(1)} %copy.30), channel_id=1, source_target_pairs={{0,16},{16,32},{32,48},{48,64},{64,80},{80,96},{96,112},{112,128},... | collective-permute-start | bytes 27656 | tf_op jit(solution)/shard_map/ppermute | solution.py:18
  264.2 13.3 %copy-start.7 = (f32[12,96,128]{2,1,0:T(8,128)S(1)}, f32[12,96,128]{2,1,0:T(8,128)}, u32[]{:S(2)}) copy-start(f32[12,96,128]{2,1,0:T(8,128)} %copy-done.6) | copy-start | bytes 1769476
  264.2 13.3 %copy-start.34 = (f32[96]{0:T(128)S(1)}, f32[96]{0:T(128)}, u32[]{:S(2)}) copy-start(f32[96]{0:T(128)} %copy-done.33) | copy-start | bytes 1156
  265.4 6.9 %collective-permute-start.10 = (f32[24,1,130]{2,1,0:T(1,128)S(1)}, f32[24,1,130]{2,1,0:T(1,128)S(1)}, u32[]{:S(2)}, u32[]{:S(2)}) collective-permute-start(f32[24,1,130]{2,1,0:T(1,128)S(1)} %get-tuple-element.21), channel_id=1, source_target_pairs={{1,0},{2,1},{3,2},{4,3},{5,4},{6,5},{7,6},{8,7},{9,8},{10,9},{11,1... | collective-permute-start | bytes 37448 | tf_op jit(solution)/shard_map/ppermute | solution.py:19
  270.3 8.2 %copy-start.39 = (f32[6]{0:T(128)S(1)}, f32[6]{0:T(128)}, u32[]{:S(2)}) copy-start(f32[6]{0:T(128)} %constant.32) | copy-start | bytes 76
  270.3 7.3 %collective-permute-start.11 = (f32[24,1,130]{2,1,0:T(1,128)S(1)}, f32[24,1,130]{2,1,0:T(1,128)S(1)}, u32[]{:S(2)}, u32[]{:S(2)}) collective-permute-start(f32[24,1,130]{2,1,0:T(1,128)S(1)} %get-tuple-element.22), channel_id=1, source_target_pairs={{0,1},{1,2},{2,3},{3,4},{4,5},{5,6},{6,7},{7,8},{8,9},{9,10},{10,1... | collective-permute-start | bytes 37448 | tf_op jit(solution)/shard_map/ppermute | solution.py:18
  278.5 0.8 copy-start.16
